TPU v7x, 256 devices: a whole 4x4x8 slice. The times are simulated.
256 devices in a mesh: opair: 8 (over y, core), vpair: 32 (over z, x).
Axes of the slice: x: 4, y: 4, z: 8, core: 2. Of those that a mesh axis runs over, the one named last changes fastest.
Arguments:
- amplitudes: bfloat16 [1600, 24, 1000], P('vpair', 'opair'), may hold values from -6 to 6
- ladder_ints: bfloat16 [24, 1000, 32, 1000], P('opair', None, 'vpair'), may hold values from -0.0390625 to 0.0390625
- cycle_amps: bfloat16 [24, 100, 512], P('opair'), may hold values from -6 to 6
- cycle_ints: bfloat16 [24, 100, 100000], P('opair', None, 'vpair'), may hold values from -0.125 to 0.125
- occ_blocks: int32 [8], replicated, may hold values from 1 to 33, 100 in all
- virt_blocks: int32 [8], replicated, may hold values from 1 to 250, 1000 in all
- occ_start: int32 [1], replicated, may hold values from 0 to 84
- virt_start: int32 [1], replicated, may hold values from 0 to 968
- eps_occ: float32 [100], replicated, may hold values from -1 to -0.25
- eps_virt: float32 [1000], replicated, may hold values from 0.25 to 1.5
Outputs:
- update: float32 [16, 32, 100, 1000], P('opair', 'vpair')
All inputs are finite; a program needn't handle non-finite values.
Results may differ from a plain program's by a relative error of at most 0.0004.
Values may be sent and summed in bfloat16 or wider, within the bound.
No kernel may reach another device: no remote copies, remote signals or barrier semaphores. Data moves between devices by JAX's collectives and lax.ppermute only.
A program may use at most 128 MiB of HBM per device.

v0:
```python
import jax
import jax.numpy as jnp
from jax import lax
from jax.sharding import PartitionSpec as P

NO = 100
NV = 1000
I_DEV = 2
A_DEV = 1
N_CHUNK = 2


def irrep_of(blocks, index):
    bounds = jnp.cumsum(blocks)[:-1]
    return jnp.sum((index[:, None] >= bounds[None, :]).astype(jnp.int32), axis=1)


def shards(
    amplitudes,
    ladder_ints,
    cycle_amps,
    cycle_ints,
    occ_blocks,
    virt_blocks,
    occ_start,
    virt_start,
    eps_occ,
    eps_virt,
):
    i_win = I_DEV * lax.axis_size("opair")
    a_win = A_DEV * lax.axis_size("vpair")
    slab_depth = ladder_ints.shape[0] * ladder_ints.shape[1]
    jb_dev = cycle_ints.shape[2]
    cycle = lax.dot_general(
        cycle_amps, cycle_ints, (((0, 1), (0, 1)), ((), ())), preferred_element_type=jnp.float32
    )
    cycle_part = cycle.reshape(i_win, a_win, jb_dev)
    c_dev = ladder_ints.shape[0]
    v_slab = ladder_ints.reshape(c_dev, ladder_ints.shape[1], A_DEV * NV)
    p_dev = amplitudes.shape[0]
    p_chunk = p_dev // N_CHUNK
    parts = []
    prev = None
    for s in range(N_CHUNK):
        loc = amplitudes[s * p_chunk : (s + 1) * p_chunk].transpose(1, 0, 2)
        if prev is None:
            loc, cycle_part = lax.optimization_barrier((loc, cycle_part))
            cycle = lax.psum_scatter(cycle_part, "opair", scatter_dimension=0, tiled=True)
        elif s == 1:
            loc, _, cycle = lax.optimization_barrier((loc, prev, cycle))
        else:
            loc, _ = lax.optimization_barrier((loc, prev))
        piece = lax.all_gather(loc, "vpair", axis=1, tiled=True)
        prev = piece
        part = lax.dot_general(
            piece, v_slab, (((0, 2), (0, 1)), ((), ())), preferred_element_type=jnp.float32
        )
        part = part.reshape(i_win, NO // N_CHUNK, A_DEV * NV)
        if s == 1:
            cycle = lax.all_to_all(cycle, "vpair", split_axis=1, concat_axis=2, tiled=True)
            part, parts[-1], cycle = lax.optimization_barrier((part, parts[-1], cycle))
        elif parts:
            part, parts[-1] = lax.optimization_barrier((part, parts[-1]))
        parts.append(lax.psum_scatter(part, "opair", scatter_dimension=0, tiled=True))
    parts = [q.reshape(I_DEV, NO // p_dev, p_chunk, A_DEV * NV) for q in parts]
    ladder = jnp.stack(parts, axis=2).reshape(I_DEV, NO, A_DEV * NV)
    resid = ladder.reshape(I_DEV, NO, A_DEV, NV).transpose(0, 2, 1, 3) + cycle.reshape(
        I_DEV, A_DEV, NO, NV
    )
    first_occ = occ_start[0] + lax.axis_index("opair") * I_DEV
    first_virt = virt_start[0] + lax.axis_index("vpair") * A_DEV
    glob_i = first_occ + jnp.arange(I_DEV, dtype=jnp.int32)
    glob_a = first_virt + jnp.arange(A_DEV, dtype=jnp.int32)
    sym_i = irrep_of(occ_blocks, glob_i)
    sym_a = irrep_of(virt_blocks, glob_a)
    sym_j = irrep_of(occ_blocks, jnp.arange(NO, dtype=jnp.int32))
    sym_b = irrep_of(virt_blocks, jnp.arange(NV, dtype=jnp.int32))
    total_sym = jnp.bitwise_xor(
        jnp.bitwise_xor(sym_i[:, None, None, None], sym_a[None, :, None, None]),
        jnp.bitwise_xor(sym_j[None, None, :, None], sym_b[None, None, None, :]),
    )
    e_i = lax.dynamic_slice_in_dim(eps_occ, first_occ, I_DEV)
    e_a = lax.dynamic_slice_in_dim(eps_virt, first_virt, A_DEV)
    denom = (
        e_i[:, None, None, None]
        - e_a[None, :, None, None]
        + eps_occ[None, None, :, None]
        - eps_virt[None, None, None, :]
    )
    return jnp.where(total_sym == 0, resid / denom, jnp.float32(0.0))


def solution(mesh):
    placed = (
        P("vpair", "opair", None),
        P("opair", None, "vpair", None),
        P("opair", None, None),
        P("opair", None, "vpair"),
        P(),
        P(),
        P(),
        P(),
        P(),
        P(),
    )
    return jax.shard_map(
        shards,
        mesh=mesh,
        in_specs=placed,
        out_specs=P("opair", "vpair", None, None),
        check_vma=False,
    )
```

profile of v0, /device:TPU:2, one launch (start us, length us, event | category | flops | bytes accessed | tf_op | source)
XLA Modules:
  0.0 265.2 jit_solution(7617233664805227034)
XLA Ops:
  7.4 1.2 fusion.19
  8.6 0.8 copy.72
  9.4 5.7 %fusion.20 = f32[512,3125,1]{1,0,2:T(8,128)} fusion(bf16[3,100,512]{2,1,0:T(8,128)(2,1)} %param.12, bf16[3,100,3125]{2,1,0:T(8,128)(2,1)S(1)} %copy-done), kind=kOutput, calls=%fused_computation.30 | convolution fusion | flops 960000000 | bytes 8582200 | tf_op jit(solution)/shard_map/dot_general | solution.py:34
  15.2 0.5 reduce-scatter.4.cloned.1.call-update
  15.7 0.8 copy.73
  16.6 89.8 %all-gather.3.cloned.1.call-done = bf16[3,800,1000]{2,0,1:T(4,128)(2,1)} async-done(((bf16[3,25,1000]{2,0,1:T(4,128)(2,1)}), bf16[3,800,1000]{2,0,1:T(4,128)(2,1)}) %all-gather.3.cloned.1.call-update) | async-done | bytes 4800016 | tf_op jit(solution)/shard_map/all_gather | solution.py:53
  106.5 13.3 %fusion.11 = f32[16,50,1000]{2,1,0:T(8,128)} fusion(bf16[3,1000,1,1000]{3,1,2,0:T(8,128)(2,1)} %param.11, bf16[16,50,3,1000]{3,2,1,0:T(4,128)(2,1)} %bitcast.55), kind=kOutput, calls=%fused_computation.7 | convolution fusion | flops 4800000000 | bytes 14000000 | tf_op jit(solution)/shard_map/dot_general | solution.py:55
  119.9 0.6 copy.43
  120.5 34.7 %all_to_all.12 = f32[2,32,3125]{2,0,1:T(2,128)S(1)} all-to-all(f32[2,32,3125]{2,0,1:T(2,128)S(1)} %copy.43), channel_id=1, replica_groups=mesh['opair'=8,'vpair'=32] {'vpair'}, dimensions={1} | all-to-all | bytes 1600000 | tf_op jit(solution)/shard_map/all_to_all | solution.py:60
  155.3 0.1 copy.44
  155.3 2.0 all_to_all.10
  157.3 43.4 %all-gather.5.cloned.1.call-done = bf16[3,800,1000]{2,0,1:T(4,128)(2,1)} async-done(((bf16[3,25,1000]{2,0,1:T(4,128)(2,1)}), bf16[3,800,1000]{2,0,1:T(4,128)(2,1)}) %all-gather.5.cloned.1.call-update) | async-done | bytes 4800016 | tf_op jit(solution)/shard_map/all_gather | solution.py:53
  200.7 13.3 %fusion.6 = f32[16,50,1000]{2,1,0:T(8,128)} fusion(bf16[3,1000,1,1000]{3,1,2,0:T(8,128)(2,1)} %param.11, bf16[16,50,3,1000]{3,2,1,0:T(4,128)(2,1)} %bitcast.56), kind=kOutput, calls=%fused_computation.6 | convolution fusion | flops 4800000000 | bytes 14000000 | tf_op jit(solution)/shard_map/dot_general | solution.py:55
  215.3 0.2 reduce-window.6
  215.5 0.2 reduce-window.9
  215.7 0.6 dynamic_slice.7
  216.4 0.7 dynamic-slice_subtract_fusion
  217.1 0.7 fusion.18
  217.8 0.1 convert_reduce_fusion
  217.9 0.1 convert_reduce_fusion.1
  218.0 0.2 fusion.17
  218.2 0.7 broadcast_xor_fusion.1
  218.9 0.1 broadcast_add_fusion
  218.9 0.1 broadcast_xor_fusion
  219.1 2.1 copy.45
  221.1 2.2 reshape.185
  223.3 28.6 %reduce-scatter.8.cloned.1.call-done = f32[2,50,1000]{2,1,0:T(8,128)} async-done(((f32[16,50,1000]{2,1,0:T(8,128)}), f32[2,50,1000]{2,1,0:T(8,128)}) %reduce-scatter.8.cloned.1.call-update) | async-done | bytes 400016 | tf_op jit(solution)/shard_map/reduce_scatter | solution.py:64
  252.0 1.3 copy.46
  253.3 1.4 pad_maximum_fusion
  254.7 0.1 copy.47
  254.8 1.1 compare_select_fusion
  255.9 1.7 copy.49
  (25 shorter events, 0.3 us)
Async XLA Ops:
  7.4 2.0 copy-start
  7.4 99.0 %all-gather.3.cloned.1.call-start = ((), (), s32[]{:S(2)}) async-start(), calls=%async_computation.4 | async-start | bytes 6758400 | tf_op jit(solution)/shard_map/all_gather | solution.py:53
  15.1 91.3 %reduce-scatter.4.cloned.1.call-start = ((), (), s32[]{:S(2)}) async-start(), calls=%async_computation.5 | async-start | bytes 7372800 | tf_op jit(solution)/shard_map/reduce_scatter | solution.py:48
  15.7 185.0 %all-gather.5.cloned.1.call-start = ((), (), s32[]{:S(2)}) async-start(), calls=%async_computation.6 | async-start | bytes 6758400 | tf_op jit(solution)/shard_map/all_gather | solution.py:53
  106.4 107.6 %reduce-scatter.6.cloned.1.call-start = ((), (), s32[]{:S(2)}) async-start(), calls=%async_computation.7 | async-start | bytes 4128768 | tf_op jit(solution)/shard_map/reduce_scatter | solution.py:64
  106.5 13.4 %copy-start.1 = (f32[2,32,3125]{2,1,0:T(8,128)S(1)}, f32[2,32,3125]{2,1,0:T(8,128)}, u32[]{:S(2)}) copy-start(f32[2,32,3125]{2,1,0:T(8,128)} %reduce-scatter.4.cloned.1.call-done) | copy-start | bytes 2400004
  119.8 132.2 %reduce-scatter.8.cloned.1.call-start = ((), (), s32[]{:S(2)}) async-start(), calls=%async_computation.8 | async-start | bytes 4128768 | tf_op jit(solution)/shard_map/reduce_scatter | solution.py:64
  200.7 14.7 %copy-start.4 = (s32[8]{0:T(128)S(1)}, s32[8]{0:T(128)}, u32[]{:S(2)}) copy-start(s32[8]{0:T(128)} %param.14) | copy-start | bytes 100
  200.7 14.9 %copy-start.5 = (s32[8]{0:T(128)S(1)}, s32[8]{0:T(128)}, u32[]{:S(2)}) copy-start(s32[8]{0:T(128)} %param.15) | copy-start | bytes 100
  200.7 15.1 %copy-start.2 = (f32[1000]{0:T(1024)S(1)}, f32[1000]{0:T(1024)}, u32[]{:S(2)}) copy-start(f32[1000]{0:T(1024)} %param.19) | copy-start | bytes 12004
  200.7 15.7 %copy-start.3 = (f32[100]{0:T(128)S(1)}, f32[100]{0:T(128)}, u32[]{:S(2)}) copy-start(f32[100]{0:T(128)} %param.18) | copy-start | bytes 1204
Sparse Core Ops, SparseCore 0:
  15.2 91.1 all-gather.2
  109.0 91.6 all-gather.4
Sparse Core Ops, SparseCore 1:
  18.2 49.4 reduce-scatter.3
  119.9 38.6 reduce-scatter.5
  214.1 37.8 reduce-scatter.7
where the time goes:
time: 266 us; the launch traced here: 265 us
  waiting for transfers between devices  162 us (61%)
  blocking collectives  34.7 us (13%)
  matrix products  32.3 us (12%)
  between operations  16.4 us (6%)
  local copies, waits for them, and re-layouts  13.6 us (5%)
  other arithmetic  5.5 us (2%)
    all_gather x2, waiting for transfers between devices, shards(): piece = lax.all_gather(loc, 'vpair', axis=1, tiled=True)  133 us
    all_to_all x1, blocking collectives, shards(): lax.all_to_all(cycle, 'vpair', split_axis=1, concat_axis=2, tiled=True)  34.7 us
    reduce_scatter x2, waiting for transfers between devices, shards(): lax.psum_scatter(part, 'opair', scatter_dimension=0, tiled=True)  28.7 us
    dot_general x2, matrix products, shards(): lax.dot_general(piece, v_slab, (((0, 2), (0, 1)), ((), ())), preferred_el...  26.7 us
    dot_general x1, matrix products, shards(): lax.dot_general(cycle_amps, cycle_ints, (((0, 1), (0, 1)), ((), ())), pre...  5.67 us
  transfers between devices with their start and end apart: 5, of which 3 were waited for; matrix products, arithmetic and copies ran while one was open for 14% of the time, Pallas kernels for 0%

commit v1 on v0

--- a/solution.py
+++ b/solution.py
@@ -50,7 +50,9 @@
             loc, _, cycle = lax.optimization_barrier((loc, prev, cycle))
         else:
             loc, _ = lax.optimization_barrier((loc, prev))
-        piece = lax.all_gather(loc, "vpair", axis=1, tiled=True)
+        piece = jnp.concatenate(
+            lax.all_to_all(jnp.stack([loc] * lax.axis_size("vpair")), "vpair", 0, 0), axis=1
+        )
         prev = piece
         part = lax.dot_general(
             piece, v_slab, (((0, 2), (0, 1)), ((), ())), preferred_element_type=jnp.float32

time: 266 us -> 437 us (1.64)
  blocking collectives: 34.7 us -> 179 us
  local copies, waits for them, and re-layouts: 13.6 us -> 56.6 us
  waiting for transfers between devices: 162 us -> 146 us
  starting transfers between devices: 0.17 us -> 5.88 us
    all_to_all x0 -> x1, blocking collectives: none -> 152 us  [shards(): lax.all_to_all(jnp.stack([loc] * lax.axis_size('vpair')), 'vpair', 0, 0)]
    all_gather x2 -> x0, waiting for transfers between devices: 133 us -> none  [shards(): piece = lax.all_gather(loc, 'vpair', axis=1, tiled=True)]
    all_to_all x0 -> x1, waiting for transfers between devices: none -> 118 us  [shards(): lax.all_to_all(jnp.stack([loc] * lax.axis_size('vpair')), 'vpair', 0, 0)]
    reshape x0 -> x4, local copies, waits for them, and re-layouts: none -> 25 us  [shards(): jnp.concatenate(lax.all_to_all(jnp.stack([loc] * lax.axis_size('vpair')),...]
    dot_general x0 -> x2, local copies, waits for them, and re-layouts: none -> 13.5 us  [shards(): lax.dot_general(piece, v_slab, (((0, 2), (0, 1)), ((), ())), preferred_el...]
    all_to_all x1, blocking collectives: 34.7 us -> 27.5 us  [shards(): lax.all_to_all(cycle, 'vpair', split_axis=1, concat_axis=2, tiled=True)]
    all_to_all x0 -> x1, starting transfers between devices: none -> 5.61 us  [shards(): lax.all_to_all(jnp.stack([loc] * lax.axis_size('vpair')), 'vpair', 0, 0)]
  transfers between devices with their start and end apart: 5 -> 4, of which waited for: 3 -> 2; matrix products, arithmetic and copies ran while one was open for 14% -> 16% of each run, Pallas kernels for 0% -> 0%
where the time goes in v1:
time: 437 us; the launch traced here: 436 us
  blocking collectives  179 us (41%)
  waiting for transfers between devices  146 us (33%)
  local copies, waits for them, and re-layouts  56.6 us (13%)
  matrix products  28 us (6%)
  between operations  14.5 us (3%)
  starting transfers between devices  5.88 us (1%)
  other arithmetic  5.5 us (1%)
    all_to_all x1, blocking collectives, shards(): lax.all_to_all(jnp.stack([loc] * lax.axis_size('vpair')), 'vpair', 0, 0)  152 us
    all_to_all x1, waiting for transfers between devices, shards(): lax.all_to_all(jnp.stack([loc] * lax.axis_size('vpair')), 'vpair', 0, 0)  118 us
    reduce_scatter x2, waiting for transfers between devices, shards(): lax.psum_scatter(part, 'opair', scatter_dimension=0, tiled=True)  28.8 us
    all_to_all x1, blocking collectives, shards(): lax.all_to_all(cycle, 'vpair', split_axis=1, concat_axis=2, tiled=True)  27.5 us
    reshape x4, local copies, waits for them, and re-layouts, shards(): jnp.concatenate(lax.all_to_all(jnp.stack([loc] * lax.axis_size('vpair')),...  25 us
    dot_general x2, matrix products, shards(): lax.dot_general(piece, v_slab, (((0, 2), (0, 1)), ((), ())), preferred_el...  22.3 us
    dot_general x2, local copies, waits for them, and re-layouts, shards(): lax.dot_general(piece, v_slab, (((0, 2), (0, 1)), ((), ())), preferred_el...  13.5 us
  transfers between devices with their start and end apart: 4, of which 2 were waited for; matrix products, arithmetic and copies ran while one was open for 16% of the time, Pallas kernels for 0%

profile of v1, /device:TPU:2, one launch (start us, length us, event | category | flops | bytes accessed | tf_op | source)
XLA Modules:
  0.0 436.2 jit_solution(7753704221787630505)
XLA Ops:
  6.5 1.2 slice_bitcast_fusion
  7.8 0.5 copy-done
  8.3 5.7 %fusion.13 = f32[512,3125,1]{1,0,2:T(8,128)} fusion(bf16[3,100,512]{2,1,0:T(8,128)(2,1)} %param.12, bf16[3,100,3125]{2,1,0:T(8,128)(2,1)S(1)} %copy-done), kind=kOutput, calls=%fused_computation.27 | convolution fusion | flops 960000000 | bytes 8582200 | tf_op jit(solution)/shard_map/dot_general | solution.py:34
  14.0 0.8 stack.6
  14.8 151.8 %all_to_all.22 = bf16[32,3,25,1000]{3,2,1,0:T(8,128)(2,1)S(1)} all-to-all(bf16[32,3,25,1000]{3,2,1,0:T(8,128)(2,1)S(1)} %stack.6), channel_id=1, replica_groups=mesh['opair'=8,'vpair'=32] {'vpair'}, dimensions={0} | all-to-all | bytes 9600000 | tf_op jit(solution)/shard_map/all_to_all | solution.py:54
  166.6 3.4 copy.37
  170.0 7.5 %reshape.201 = bf16[3,800,1000]{2,1,0:T(8,128)(2,1)} reshape(bf16[3,32,25,1000]{3,2,1,0:T(8,128)(2,1)} %copy.37) | data formatting | bytes 9600000 | tf_op jit(solution)/shard_map/reshape | solution.py:53
  177.4 1.8 copy.39
  179.2 27.5 %all_to_all.23 = f32[2,32,3125]{2,0,1:T(2,128)S(1)} all-to-all(f32[2,32,3125]{2,0,1:T(2,128)S(1)} %copy.39), channel_id=1, replica_groups=mesh['opair'=8,'vpair'=32] {'vpair'}, dimensions={1} | all-to-all | bytes 1600000 | tf_op jit(solution)/shard_map/all_to_all | solution.py:62
  206.7 3.5 stack.7
  210.1 5.6 %all-to-all-start.1 = ((bf16[32,3,25,1000]{3,2,1,0:T(8,128)(2,1)}), bf16[32,3,25,1000]{3,2,1,0:T(8,128)(2,1)}, u32[]{:S(2)}, u32[]{:S(2)}) async-start(bf16[32,3,25,1000]{3,2,1,0:T(8,128)(2,1)} %stack.7), calls=%async_computation.2 | async-start | bytes 12582912 | tf_op jit(solution)/shard_map/all_to_all | solution.py:54
  215.8 6.8 %dot_general.22 = bf16[16,50,3,1000]{3,1,0,2:T(8,128)(2,1)} reshape(bf16[800,3,1000]{2,0,1:T(8,128)(2,1)} %bitcast.53) | data formatting | bytes 9600000 | tf_op jit(solution)/shard_map/dot_general | solution.py:57
  222.6 11.1 %fusion.7 = f32[16,50,1000]{2,1,0:T(8,128)} fusion(bf16[16,50,3,1000]{3,1,0,2:T(8,128)(2,1)} %dot_general.22, bf16[3,1000,1,1000]{3,1,2,0:T(8,128)(2,1)} %param.11), kind=kOutput, calls=%fused_computation.5 | convolution fusion | flops 4800000000 | bytes 14000000 | tf_op jit(solution)/shard_map/dot_general | solution.py:57
  233.7 0.2 reduce-scatter.8.cloned.1.call-start
  234.0 2.0 all_to_all.18
  236.0 117.6 %all-to-all-done.1 = bf16[32,3,25,1000]{3,2,1,0:T(8,128)(2,1)} async-done(((bf16[32,3,25,1000]{3,2,1,0:T(8,128)(2,1)}), bf16[32,3,25,1000]{3,2,1,0:T(8,128)(2,1)}, u32[]{:S(2)}, u32[]{:S(2)}) %all-to-all-start.1) | async-done | bytes 4800032 | tf_op jit(solution)/shard_map/all_to_all | solution.py:54
  353.5 6.8 %copy.38 = bf16[3,32,25,1000]{3,2,1,0:T(8,128)(2,1)} copy(bf16[3,32,25,1000]{3,2,0,1:T(8,128)(2,1)} %bitcast.11) | data formatting | bytes 9600000 | tf_op jit(solution)/shard_map/reshape | solution.py:53
  360.3 7.4 %reshape.203 = bf16[3,800,1000]{2,1,0:T(8,128)(2,1)} reshape(bf16[3,32,25,1000]{3,2,1,0:T(8,128)(2,1)} %copy.38) | data formatting | bytes 9600000 | tf_op jit(solution)/shard_map/reshape | solution.py:53
  367.7 6.7 %dot_general.19 = bf16[16,50,3,1000]{3,1,0,2:T(8,128)(2,1)} reshape(bf16[800,3,1000]{2,0,1:T(8,128)(2,1)} %bitcast.54) | data formatting | bytes 9600000 | tf_op jit(solution)/shard_map/dot_general | solution.py:57
  374.5 11.2 %fusion.4 = f32[16,50,1000]{2,1,0:T(8,128)} fusion(bf16[16,50,3,1000]{3,1,0,2:T(8,128)(2,1)} %dot_general.19, bf16[3,1000,1,1000]{3,1,2,0:T(8,128)(2,1)} %param.11), kind=kOutput, calls=%fused_computation.4 | convolution fusion | flops 4800000000 | bytes 14000000 | tf_op jit(solution)/shard_map/dot_general | solution.py:57
  387.0 0.2 reduce-window.6
  387.4 0.6 dynamic_slice.7
  388.1 0.7 dynamic-slice_subtract_fusion
  388.8 0.7 fusion.12
  389.9 0.7 broadcast_xor_fusion.1
  390.8 2.2 copy.41
  393.0 2.2 reshape.205
  395.2 28.8 %reduce-scatter.8.cloned.1.call-done = f32[2,50,1000]{2,1,0:T(8,128)} async-done(((f32[16,50,1000]{2,1,0:T(8,128)}), f32[2,50,1000]{2,1,0:T(8,128)}) %reduce-scatter.8.cloned.1.call-update) | async-done | bytes 400016 | tf_op jit(solution)/shard_map/reduce_scatter | solution.py:66
  424.0 1.3 copy.42
  425.3 1.4 pad_maximum_fusion
  426.8 1.1 compare_select_fusion
  427.9 1.7 copy.45
  (28 shorter events, 1.0 us)
Async XLA Ops:
  6.5 1.7 copy-start
  6.5 170.9 %reduce-scatter.4.cloned.1.call-start = ((), (), s32[]{:S(2)}) async-start(), calls=%async_computation.6 | async-start | bytes 7372800 | tf_op jit(solution)/shard_map/reduce_scatter | solution.py:48
  210.1 143.4 %all-to-all-start.1 = ((bf16[32,3,25,1000]{3,2,1,0:T(8,128)(2,1)}), bf16[32,3,25,1000]{3,2,1,0:T(8,128)(2,1)}, u32[]{:S(2)}, u32[]{:S(2)}) async-start(bf16[32,3,25,1000]{3,2,1,0:T(8,128)(2,1)} %stack.7), calls=%async_computation.2 | async-start | bytes 12582912 | tf_op jit(solution)/shard_map/all_to_all | solution.py:54
  215.8 169.9 %reduce-scatter.6.cloned.1.call-start = ((), (), s32[]{:S(2)}) async-start(), calls=%async_computation.7 | async-start | bytes 4128768 | tf_op jit(solution)/shard_map/reduce_scatter | solution.py:66
  233.7 190.3 %reduce-scatter.8.cloned.1.call-start = ((), (), s32[]{:S(2)}) async-start(), calls=%async_computation.8 | async-start | bytes 4128768 | tf_op jit(solution)/shard_map/reduce_scatter | solution.py:66
  374.5 12.6 %copy-start.4 = (s32[8]{0:T(128)S(1)}, s32[8]{0:T(128)}, u32[]{:S(2)}) copy-start(s32[8]{0:T(128)} %param.14) | copy-start | bytes 100
  374.5 12.8 %copy-start.5 = (s32[8]{0:T(128)S(1)}, s32[8]{0:T(128)}, u32[]{:S(2)}) copy-start(s32[8]{0:T(128)} %param.15) | copy-start | bytes 100
  374.5 12.9 %copy-start.2 = (f32[1000]{0:T(1024)S(1)}, f32[1000]{0:T(1024)}, u32[]{:S(2)}) copy-start(f32[1000]{0:T(1024)} %param.19) | copy-start | bytes 12004
  374.5 13.6 %copy-start.3 = (f32[100]{0:T(128)S(1)}, f32[100]{0:T(128)}, u32[]{:S(2)}) copy-start(f32[100]{0:T(128)} %param.18) | copy-start | bytes 1204
  390.6 39.0 %copy-start.1 = (bf16[3,100,3125]{2,1,0:T(8,128)(2,1)S(1)}, bf16[3,100,3125]{2,1,0:T(8,128)(2,1)}, u32[]{:S(2)}) copy-start(bf16[3,100,3125]{2,1,0:T(8,128)(2,1)} %param.13) | copy-start | bytes 5625004
Sparse Core Ops, SparseCore 0:
  14.1 49.2 reduce-scatter.3
  233.8 41.5 reduce-scatter.5
  385.8 38.0 reduce-scatter.7
